TPU v7x, 128 devices: a whole 4x4x4 slice. The times are simulated.
128 devices in a mesh: grp: 8 (over y, core), shard: 16 (over z, x).
Axes of the slice: x: 4, y: 4, z: 4, core: 2. Of those that a mesh axis runs over, the one named last changes fastest.
Arguments:
- tokens: bfloat16 [65536, 2560], P(('grp', 'shard')), may hold values from -6 to 6
- gain: float32 [2560], replicated, may hold values from 0.25 to 1.75
- w_qkv: bfloat16 [2560, 3072], P(None, 'shard'), may hold values from -1 to 1
- prefix_kv: bfloat16 [8, 2048, 512], P('grp', 'shard'), may hold values from -6 to 6
- prefix_owner: int32 [8], P('grp'), may hold values from 0 to 7, as said below
- suffix_len: int32 [8, 16], P('grp', 'shard'), may hold values from 1 to 512, 5120 in all within a row
- slots: int32 [8, 8192], P('grp', 'shard'), may hold values from 0 to 8191, as said below
Outputs:
- attended: bfloat16 [65536, 2560], P(('grp', 'shard'))
Inputs may be any that keep to these rules, and one draw needn't show every extreme that they name: In each group the slots are a permutation of 0 to 8191; in each aligned run of 512 entries the k-th block of 32 entries holds slots k * 512 to (k + 1) * 512 - 1. `suffix_len`: each group's lengths sum to 5120 and one of them equals 512. `prefix_owner`: each entry names one of the 8 caches; several groups may name the same one.
All inputs are finite; a program needn't handle non-finite values.
Results may differ from a plain program's by a relative error of at most 0.0069.
Values may be sent and summed in bfloat16 or wider, within the bound.
No kernel may reach another device: no remote copies, remote signals or barrier semaphores. Data moves between devices by JAX's collectives and lax.ppermute only.
A program may use at most 128 MiB of HBM per device.

v0:
```python
import jax
import jax.numpy as jnp
from jax import lax
from jax.sharding import PartitionSpec as P

H = 10
HD = 256
WINDOW = 2048
SUF = 512
HQ = 2560


def normalize(rows, gain):
    rows32 = rows.astype(jnp.float32)
    factor = lax.rsqrt(jnp.mean(rows32 * rows32, axis=-1, keepdims=True) + 1e-06)
    return (rows32 * factor * gain).astype(jnp.bfloat16)


def attend_request(queries, suffix_kv, prefix, length):
    keys = jnp.concatenate([prefix[:, :HD], suffix_kv[:, :HD]], axis=0)
    values = jnp.concatenate([prefix[:, HD:], suffix_kv[:, HD:]], axis=0)
    span = keys.shape[0]
    prefix_len = prefix.shape[0]
    count = queries.shape[0]
    query_pos = jnp.arange(count, dtype=jnp.int32)[:, None]
    key_pos = jnp.arange(span, dtype=jnp.int32)[None, :]
    visible = (
        (key_pos > prefix_len + query_pos - WINDOW)
        & (key_pos <= prefix_len + query_pos)
        & (key_pos < prefix_len + length)
    )
    heads = queries.reshape(count, H, HD).transpose(1, 0, 2)

    def one_head(head_q):
        scores = jnp.dot(head_q, keys.T, preferred_element_type=jnp.float32) * HD ** (-0.5)
        scores = jnp.where(visible, scores, -1e30)
        top = jnp.max(scores, axis=-1, keepdims=True)
        expd = jnp.exp(scores - top)
        weights = (expd / jnp.sum(expd, axis=-1, keepdims=True)).astype(jnp.bfloat16)
        return jnp.dot(weights, values, preferred_element_type=jnp.float32)

    result = lax.map(one_head, heads).transpose(1, 0, 2).reshape(count, H * HD)
    return jnp.where(query_pos < length, result, 0.0).astype(jnp.bfloat16)


def shards(tokens, gain, w_qkv, prefix_kv, prefix_owner, suffix_len, slots):
    tok_dev = tokens.shape[0]
    order = slots.reshape(tok_dev)
    normed = normalize(tokens, gain)
    projected = jnp.dot(
        normed,
        lax.all_gather(w_qkv, "shard", axis=1, tiled=True),
        preferred_element_type=jnp.float32,
    ).astype(jnp.bfloat16)
    arrived, order = (
        lax.all_to_all(projected, "shard", split_axis=0, concat_axis=0, tiled=True),
        lax.all_to_all(order, "shard", split_axis=0, concat_axis=0, tiled=True),
    )
    first_slot = lax.axis_index("shard") * tok_dev
    placed = jnp.zeros_like(arrived).at[order - first_slot].set(arrived)
    owner = prefix_owner[0]
    sliced = lax.all_gather(prefix_kv, "grp", axis=0, tiled=True)
    chosen = lax.dynamic_index_in_dim(sliced, owner, 0, keepdims=False)
    prefix = lax.all_gather(chosen, "shard", axis=0, tiled=True)
    lengths = suffix_len.reshape(-1)
    req_count = lengths.shape[0]
    blocks = placed.reshape(req_count, SUF, placed.shape[1])
    results = attend_request(blocks[0, :, :HQ], blocks[0, :, HQ:], prefix, lengths[0])
    return results


def solution(mesh):
    return jax.shard_map(
        shards,
        mesh=mesh,
        in_specs=(
            P(("grp", "shard"), None),
            P(),
            P(None, "shard"),
            P("grp", "shard", None),
            P("grp"),
            P("grp", "shard"),
            P("grp", "shard"),
        ),
        out_specs=P(("grp", "shard"), None),
        check_vma=False,
    )
```

profile of v0, /device:TPU:1, one launch (start us, length us, event | category | flops | bytes accessed | tf_op | source)
XLA Modules:
  0.0 314.7 jit_solution(14929914385447946524)
XLA Ops:
  10.6 8.4 %all-to-all-start = ((s32[16,32,1]{1,2,0:T(1,128)}), s32[16,32,1]{1,2,0:T(1,128)S(1)}, u32[]{:S(2)}, u32[]{:S(2)}) async-start(s32[16,32,1]{1,2,0:T(1,128)} %all_to_all.14), calls=%async_computation | async-start | bytes 16384 | tf_op jit(solution)/shard_map/all_to_all | solution.py:57
  19.7 2.4 fusion.11
  22.0 13.9 %all-gather.7.cloned.1.call-done = bf16[8,128,512]{2,1,0:T(8,128)(2,1)} async-done(((bf16[1,128,512]{2,1,0:T(8,128)(2,1)}), bf16[8,128,512]{2,1,0:T(8,128)(2,1)}) %all-gather.7.cloned.1.call-update) | async-done | bytes 1048592 | tf_op jit(solution)/shard_map/all_gather | solution.py:62
  37.5 106.0 %all-gather.5.cloned.1.call-done = bf16[2560,3072]{0,1:T(8,128)(2,1)} async-done(((bf16[2560,192]{0,1:T(8,128)(2,1)}), bf16[2560,3072]{0,1:T(8,128)(2,1)}) %all-gather.5.cloned.1.call-update) | async-done | bytes 15728656 | tf_op jit(solution)/shard_map/all_gather | solution.py:52
  143.5 13.0 %convolution_convert_fusion = bf16[512,3072]{1,0:T(8,128)(2,1)} fusion(bf16[2560,3072]{0,1:T(8,128)(2,1)} %all-gather.5.cloned.1.call-done, bf16[512,2560]{1,0:T(8,128)(2,1)S(1)} %copy-done.3, f32[2560]{0:T(1024)S(1)} %copy-done.5, f32[512]{0:T(512)S(1)} %add_rsqrt_fusion), kind=kOutput, calls=%fused_computation.23 | convolution fusion | flops 8059879424 | bytes 21508096 | tf_op jit(solution)/shard_map/dot_general | solution.py:50
  156.5 5.0 %all-to-all-start.1 = ((bf16[16,32,3072]{2,1,0:T(8,128)(2,1)}), bf16[16,32,3072]{2,1,0:T(8,128)(2,1)S(1)}, u32[]{:S(2)}, u32[]{:S(2)}) async-start(bf16[16,32,3072]{2,1,0:T(8,128)(2,1)} %bitcast.2), calls=%async_computation.1 | async-start | bytes 6291456 | tf_op jit(solution)/shard_map/all_to_all | solution.py:56
  162.3 53.6 %all-gather.9.cloned.1.call-done = bf16[1,2048,512]{2,1,0:T(8,128)(2,1)} async-done(((bf16[1,128,512]{2,1,0:T(8,128)(2,1)}), bf16[1,2048,512]{2,1,0:T(8,128)(2,1)}) %all-gather.9.cloned.1.call-update) | async-done | bytes 2097168 | tf_op jit(solution)/shard_map/all_gather | solution.py:64
  215.9 3.0 fusion.21
  220.6 7.3 %scatter_custom_fusion = bf16[512,3072]{1,0:T(8,128)(2,1)S(1)} fusion(s32[512]{0:T(512)S(1)} %bitcast.50, bf16[512,3072]{1,0:T(8,128)(2,1)} %bitcast.47, bf16[]{:T(256)} %constant.11.clone.1), kind=kCustom, calls=%fused_computation.26 | custom fusion | bytes 3146240 | tf_op jit(solution)/shard_map/scatter | solution.py:60
  230.4 4.5 %copy.20 = bf16[1,512,2560]{1,2,0:T(8,128)(2,1)} copy(bf16[1,512,2560]{2,1,0:T(8,128)(2,1)} %slice.24) | data formatting | bytes 5242880 | tf_op jit(solution)/shard_map/slice | solution.py:68
  235.0 2.3 pad_maximum_fusion
  237.2 65.9 %while.11 = (s32[]{:T(128)}, bf16[10,512,256]{1,2,0:T(8,128)(2,1)}, bf16[10,512,256]{1,2,0:T(8,128)(2,1)}, bf16[2560,256]{1,0:T(8,128)(2,1)S(1)}, bf16[2560,256]...) while((s32[]{:T(128)}, bf16[10,512,256]{1,2,0:T(8,128)(2,1)}, ...), condition=%wide.region_5.6_spmd.clone, body=%wide.region_2.5_spmd.clone.sunk | while | flops 1357904896 | bytes 24395376 | solution.py:42
  237.2 3.2 %fusion.33 = (f32[512]{0:T(512)S(1)}, f32[512,2560]{1,0:T(8,128)S(1)}) fusion(bf16[2560,256]{1,0:T(8,128)(2,1)S(1)} %get-tuple-element.165, bf16[10,512,256]{1,2,0:T(8,128)(2,1)} %get-tuple-element.164, s32[]{:T(128)} %get-tuple-element.154, pred[2560]{0:T(1024)(128)(4,1)S(1)} %get-tuple-element.168, s32[512]{0:T(512)S(1)} %get-tuple-element.167), kind=kOutput, calls=%fused_computation.38.clone.1 | convolution fusion | flops 680263168 | bytes 6822912 | tf_op jit(solution)/shard_map/while/body/eval_jaxpr/dot_general | solution.py:35
  243.8 3.2 %fusion.33 = (f32[512]{0:T(512)S(1)}, f32[512,2560]{1,0:T(8,128)S(1)}) fusion(bf16[2560,256]{1,0:T(8,128)(2,1)S(1)} %get-tuple-element.165, bf16[10,512,256]{1,2,0:T(8,128)(2,1)} %get-tuple-element.164, s32[]{:T(128)} %get-tuple-element.154, pred[2560]{0:T(1024)(128)(4,1)S(1)} %get-tuple-element.168, s32[512]{0:T(512)S(1)} %get-tuple-element.167), kind=kOutput, calls=%fused_computation.38.clone.1 | convolution fusion | flops 680263168 | bytes 6822912 | tf_op jit(solution)/shard_map/while/body/eval_jaxpr/dot_general | solution.py:35
  250.4 3.2 %fusion.33 = (f32[512]{0:T(512)S(1)}, f32[512,2560]{1,0:T(8,128)S(1)}) fusion(bf16[2560,256]{1,0:T(8,128)(2,1)S(1)} %get-tuple-element.165, bf16[10,512,256]{1,2,0:T(8,128)(2,1)} %get-tuple-element.164, s32[]{:T(128)} %get-tuple-element.154, pred[2560]{0:T(1024)(128)(4,1)S(1)} %get-tuple-element.168, s32[512]{0:T(512)S(1)} %get-tuple-element.167), kind=kOutput, calls=%fused_computation.38.clone.1 | convolution fusion | flops 680263168 | bytes 6822912 | tf_op jit(solution)/shard_map/while/body/eval_jaxpr/dot_general | solution.py:35
  257.0 3.2 %fusion.33 = (f32[512]{0:T(512)S(1)}, f32[512,2560]{1,0:T(8,128)S(1)}) fusion(bf16[2560,256]{1,0:T(8,128)(2,1)S(1)} %get-tuple-element.165, bf16[10,512,256]{1,2,0:T(8,128)(2,1)} %get-tuple-element.164, s32[]{:T(128)} %get-tuple-element.154, pred[2560]{0:T(1024)(128)(4,1)S(1)} %get-tuple-element.168, s32[512]{0:T(512)S(1)} %get-tuple-element.167), kind=kOutput, calls=%fused_computation.38.clone.1 | convolution fusion | flops 680263168 | bytes 6822912 | tf_op jit(solution)/shard_map/while/body/eval_jaxpr/dot_general | solution.py:35
  263.6 3.2 %fusion.33 = (f32[512]{0:T(512)S(1)}, f32[512,2560]{1,0:T(8,128)S(1)}) fusion(bf16[2560,256]{1,0:T(8,128)(2,1)S(1)} %get-tuple-element.165, bf16[10,512,256]{1,2,0:T(8,128)(2,1)} %get-tuple-element.164, s32[]{:T(128)} %get-tuple-element.154, pred[2560]{0:T(1024)(128)(4,1)S(1)} %get-tuple-element.168, s32[512]{0:T(512)S(1)} %get-tuple-element.167), kind=kOutput, calls=%fused_computation.38.clone.1 | convolution fusion | flops 680263168 | bytes 6822912 | tf_op jit(solution)/shard_map/while/body/eval_jaxpr/dot_general | solution.py:35
  270.2 3.2 %fusion.33 = (f32[512]{0:T(512)S(1)}, f32[512,2560]{1,0:T(8,128)S(1)}) fusion(bf16[2560,256]{1,0:T(8,128)(2,1)S(1)} %get-tuple-element.165, bf16[10,512,256]{1,2,0:T(8,128)(2,1)} %get-tuple-element.164, s32[]{:T(128)} %get-tuple-element.154, pred[2560]{0:T(1024)(128)(4,1)S(1)} %get-tuple-element.168, s32[512]{0:T(512)S(1)} %get-tuple-element.167), kind=kOutput, calls=%fused_computation.38.clone.1 | convolution fusion | flops 680263168 | bytes 6822912 | tf_op jit(solution)/shard_map/while/body/eval_jaxpr/dot_general | solution.py:35
  276.8 3.2 %fusion.33 = (f32[512]{0:T(512)S(1)}, f32[512,2560]{1,0:T(8,128)S(1)}) fusion(bf16[2560,256]{1,0:T(8,128)(2,1)S(1)} %get-tuple-element.165, bf16[10,512,256]{1,2,0:T(8,128)(2,1)} %get-tuple-element.164, s32[]{:T(128)} %get-tuple-element.154, pred[2560]{0:T(1024)(128)(4,1)S(1)} %get-tuple-element.168, s32[512]{0:T(512)S(1)} %get-tuple-element.167), kind=kOutput, calls=%fused_computation.38.clone.1 | convolution fusion | flops 680263168 | bytes 6822912 | tf_op jit(solution)/shard_map/while/body/eval_jaxpr/dot_general | solution.py:35
  283.4 3.2 %fusion.33 = (f32[512]{0:T(512)S(1)}, f32[512,2560]{1,0:T(8,128)S(1)}) fusion(bf16[2560,256]{1,0:T(8,128)(2,1)S(1)} %get-tuple-element.165, bf16[10,512,256]{1,2,0:T(8,128)(2,1)} %get-tuple-element.164, s32[]{:T(128)} %get-tuple-element.154, pred[2560]{0:T(1024)(128)(4,1)S(1)} %get-tuple-element.168, s32[512]{0:T(512)S(1)} %get-tuple-element.167), kind=kOutput, calls=%fused_computation.38.clone.1 | convolution fusion | flops 680263168 | bytes 6822912 | tf_op jit(solution)/shard_map/while/body/eval_jaxpr/dot_general | solution.py:35
  290.0 3.2 %fusion.33 = (f32[512]{0:T(512)S(1)}, f32[512,2560]{1,0:T(8,128)S(1)}) fusion(bf16[2560,256]{1,0:T(8,128)(2,1)S(1)} %get-tuple-element.165, bf16[10,512,256]{1,2,0:T(8,128)(2,1)} %get-tuple-element.164, s32[]{:T(128)} %get-tuple-element.154, pred[2560]{0:T(1024)(128)(4,1)S(1)} %get-tuple-element.168, s32[512]{0:T(512)S(1)} %get-tuple-element.167), kind=kOutput, calls=%fused_computation.38.clone.1 | convolution fusion | flops 680263168 | bytes 6822912 | tf_op jit(solution)/shard_map/while/body/eval_jaxpr/dot_general | solution.py:35
  296.6 3.2 %fusion.33 = (f32[512]{0:T(512)S(1)}, f32[512,2560]{1,0:T(8,128)S(1)}) fusion(bf16[2560,256]{1,0:T(8,128)(2,1)S(1)} %get-tuple-element.165, bf16[10,512,256]{1,2,0:T(8,128)(2,1)} %get-tuple-element.164, s32[]{:T(128)} %get-tuple-element.154, pred[2560]{0:T(1024)(128)(4,1)S(1)} %get-tuple-element.168, s32[512]{0:T(512)S(1)} %get-tuple-element.167), kind=kOutput, calls=%fused_computation.38.clone.1 | convolution fusion | flops 680263168 | bytes 6822912 | tf_op jit(solution)/shard_map/while/body/eval_jaxpr/dot_general | solution.py:35
  303.2 2.2 fusion.14
  305.4 2.8 copy.23
  (73 shorter events, 43.3 us)
Async XLA Ops:
  6.5 137.0 %copy-start.3 = (bf16[512,2560]{1,0:T(8,128)(2,1)S(1)}, bf16[512,2560]{1,0:T(8,128)(2,1)}, u32[]{:S(2)}) copy-start(bf16[512,2560]{1,0:T(8,128)(2,1)} %param.9) | copy-start | bytes 7864324
  6.5 137.0 %copy-start.5 = (f32[2560]{0:T(1024)S(1)}, f32[2560]{0:T(1024)}, u32[]{:S(2)}) copy-start(f32[2560]{0:T(1024)} %param.10) | copy-start | bytes 30724
  6.5 29.4 %all-gather.7.cloned.1.call-start = ((), (), s32[]{:S(2)}) async-start(), calls=%async_computation.3 | async-start | bytes 1179648 | tf_op jit(solution)/shard_map/all_gather | solution.py:62
  7.3 136.2 %all-gather.5.cloned.1.call-start = ((), (), s32[]{:S(2)}) async-start(), calls=%async_computation.2 | async-start | bytes 16711680 | tf_op jit(solution)/shard_map/all_gather | solution.py:52
  10.6 145.9 %all-to-all-start = ((s32[16,32,1]{1,2,0:T(1,128)}), s32[16,32,1]{1,2,0:T(1,128)S(1)}, u32[]{:S(2)}, u32[]{:S(2)}) async-start(s32[16,32,1]{1,2,0:T(1,128)} %all_to_all.14), calls=%async_computation | async-start | bytes 16384 | tf_op jit(solution)/shard_map/all_to_all | solution.py:57
  19.0 196.9 %all-gather.9.cloned.1.call-start = ((), (), s32[]{:S(2)}) async-start(), calls=%async_computation.4 | async-start | bytes 2228224 | tf_op jit(solution)/shard_map/all_gather | solution.py:64
  156.5 62.4 %all-to-all-start.1 = ((bf16[16,32,3072]{2,1,0:T(8,128)(2,1)}), bf16[16,32,3072]{2,1,0:T(8,128)(2,1)S(1)}, u32[]{:S(2)}, u32[]{:S(2)}) async-start(bf16[16,32,3072]{2,1,0:T(8,128)(2,1)} %bitcast.2), calls=%async_computation.1 | async-start | bytes 6291456 | tf_op jit(solution)/shard_map/all_to_all | solution.py:56
  218.9 1.6 copy-start.2
  230.4 4.5 %copy-start = (bf16[2048,256]{1,0:T(8,128)(2,1)S(1)}, bf16[2048,256]{1,0:T(8,128)(2,1)}, u32[]{:S(2)}) copy-start(bf16[2048,256]{1,0:T(8,128)(2,1)} %get-tuple-element.93) | copy-start | bytes 3145732
  230.4 4.5 %copy-start.1 = (bf16[2048,256]{1,0:T(8,128)(2,1)S(1)}, bf16[2048,256]{1,0:T(8,128)(2,1)}, u32[]{:S(2)}) copy-start(bf16[2048,256]{1,0:T(8,128)(2,1)} %get-tuple-element.94) | copy-start | bytes 3145732
  240.5 1.3 copy-start.4
  247.1 1.3 copy-start.4
  253.7 1.3 copy-start.4
  260.2 1.3 copy-start.4
  266.8 1.3 copy-start.4
  273.4 1.3 copy-start.4
  280.0 1.3 copy-start.4
  286.6 1.3 copy-start.4
  293.2 1.3 copy-start.4
  299.8 1.3 copy-start.4
Sparse Core Ops, SparseCore 0:
  9.0 26.8 all-gather.6
  38.1 105.3 all-gather.4
  145.6 70.2 all-gather.8
where the time goes:
time: 316 us; the launch traced here: 315 us
  waiting for transfers between devices  175 us (55%)
  matrix products  65.7 us (21%)
  local copies, waits for them, and re-layouts  29.4 us (9%)
  other arithmetic  16.6 us (5%)
  between operations  14.5 us (5%)
  starting transfers between devices  13.5 us (4%)
    all_gather x1, waiting for transfers between devices, shards(): lax.all_gather(w_qkv, 'shard', axis=1, tiled=True)  106 us
    all_gather x1, waiting for transfers between devices, shards(): prefix = lax.all_gather(chosen, 'shard', axis=0, tiled=True)  53.6 us
    dot_general x10, matrix products, one_head(): jnp.dot(head_q, keys.T, preferred_element_type=jnp.float32) * HD ** (-0.5)  32.5 us
    dot_general x10, matrix products, one_head(): return jnp.dot(weights, values, preferred_element_type=jnp.float32)  20.2 us
    all_gather x1, waiting for transfers between devices, shards(): sliced = lax.all_gather(prefix_kv, 'grp', axis=0, tiled=True)  13.9 us
    dot_general x1, matrix products, shards(): jnp.dot(normed, lax.all_gather(w_qkv, 'shard', axis=1, tiled=True), prefe...  13 us
    all_to_all x1, starting transfers between devices, shards(): lax.all_to_all(order, 'shard', split_axis=0, concat_axis=0, tiled=True)  8.42 us
    reduce_sum x10, other arithmetic, one_head(): jnp.sum(expd, axis=-1, keepdims=True)  8.39 us
  transfers between devices with their start and end apart: 5, of which 3 were waited for; matrix products, arithmetic and copies ran while one was open for 7% of the time, Pallas kernels for 0%

commit v1 on v0

--- a/solution.py
+++ b/solution.py
@@ -8,6 +8,42 @@
 WINDOW = 2048
 SUF = 512
 HQ = 2560
+
+
+def define_seats_all(frame_in, at_axis):
+    frame_in = jnp.moveaxis(frame_in, 0, at_axis)
+    main = frame_in.shape
+    return frame_in.reshape(
+        *main[:at_axis], main[at_axis] * main[at_axis + 1], *main[at_axis + 2 :]
+    )
+
+
+def run_copies_on_mesh(out_dim, across, local_block):
+    k_all = lax.axis_size(across)
+    arrivals = []
+    no = 0
+    while no < k_all:
+        arrivals.append((no, (no + 1) % k_all))
+        no = no + 1
+    so_far_all = []
+    for i0, k in arrivals:
+        so_far_all.append((k, i0))
+    b_next, after = ([], [])
+    p = 0
+    while p < k_all - 1:
+        if p % 2 == 0:
+            res = lax.ppermute(b_next[-1] if b_next else local_block, across, arrivals)
+            b_next.append(res)
+        else:
+            response = lax.ppermute(after[-1] if after else local_block, across, so_far_all)
+            after.append(response)
+        p = p + 1
+    inter = jnp.stack([*b_next[::-1], local_block, *after], 0)
+    m_next = lax.axis_index(across)
+    x_next = len(b_next)
+    next_value = m_next - x_next
+    inter = inter[(jnp.arange(k_all) - next_value) % k_all]
+    return define_seats_all(inter, out_dim)
 
 
 def normalize(rows, gain):
@@ -59,7 +95,7 @@
     first_slot = lax.axis_index("shard") * tok_dev
     placed = jnp.zeros_like(arrived).at[order - first_slot].set(arrived)
     owner = prefix_owner[0]
-    sliced = lax.all_gather(prefix_kv, "grp", axis=0, tiled=True)
+    sliced = run_copies_on_mesh(0, "grp", prefix_kv)
     chosen = lax.dynamic_index_in_dim(sliced, owner, 0, keepdims=False)
     prefix = lax.all_gather(chosen, "shard", axis=0, tiled=True)
     lengths = suffix_len.reshape(-1)

time: 316 us -> 290 us (0.918)
  waiting for transfers between devices: 175 us -> 129 us
  starting transfers between devices: 13.5 us -> 25.1 us
  local copies, waits for them, and re-layouts: 29.4 us -> 37.6 us
    all_gather x1, waiting for transfers between devices: 106 us -> 73.5 us  [shards(): lax.all_gather(w_qkv, 'shard', axis=1, tiled=True)]
    all_gather x1 -> x0, waiting for transfers between devices: 13.9 us -> none  [shards(): sliced = lax.all_gather(prefix_kv, 'grp', axis=0, tiled=True)]
    ppermute x0 -> x7, starting transfers between devices: none -> 12.5 us  [the longest x4 8.74 us: run_copies_on_mesh(): res = lax.ppermute(b_next[-1] if b_next else local_block, across, arrivals)]
    unnamed x11 -> x23, local copies, waits for them, and re-layouts: 2.17 us -> 8.36 us
  transfers between devices with their start and end apart: 5 -> 11, of which waited for: 3 -> 3; matrix products, arithmetic and copies ran while one was open for 7% -> 11% of each run, Pallas kernels for 0% -> 0%
where the time goes in v1:
time: 290 us; the launch traced here: 289 us
  waiting for transfers between devices  129 us (44%)
  matrix products  65.7 us (23%)
  local copies, waits for them, and re-layouts  37.6 us (13%)
  starting transfers between devices  25.1 us (9%)
  other arithmetic  17.1 us (6%)
  between operations  14.8 us (5%)
    all_gather x1, waiting for transfers between devices, shards(): lax.all_gather(w_qkv, 'shard', axis=1, tiled=True)  73.5 us
    all_gather x1, waiting for transfers between devices, shards(): prefix = lax.all_gather(chosen, 'shard', axis=0, tiled=True)  53.5 us
    dot_general x10, matrix products, one_head(): jnp.dot(head_q, keys.T, preferred_element_type=jnp.float32) * HD ** (-0.5)  32.4 us
    dot_general x10, matrix products, one_head(): return jnp.dot(weights, values, preferred_element_type=jnp.float32)  20.2 us
    dot_general x1, matrix products, shards(): jnp.dot(normed, lax.all_gather(w_qkv, 'shard', axis=1, tiled=True), prefe...  13 us
    ppermute x4, starting transfers between devices, run_copies_on_mesh(): res = lax.ppermute(b_next[-1] if b_next else local_block, across, arrivals)  8.74 us
    reduce_sum x10, other arithmetic, one_head(): jnp.sum(expd, axis=-1, keepdims=True)  8.39 us
    unnamed x23, local copies, waits for them, and re-layouts  8.36 us
  transfers between devices with their start and end apart: 11, of which 3 were waited for; matrix products, arithmetic and copies ran while one was open for 11% of the time, Pallas kernels for 0%

profile of v1, /device:TPU:1, one launch (start us, length us, event | category | flops | bytes accessed | tf_op | source)
XLA Modules:
  0.0 289.0 jit_solution(17334438274319289056)
XLA Ops:
  7.3 2.7 collective-permute-start
  12.5 7.6 %all-to-all-start = ((s32[16,32,1]{1,2,0:T(1,128)}), s32[16,32,1]{1,2,0:T(1,128)S(1)}, u32[]{:S(2)}, u32[]{:S(2)}) async-start(s32[16,32,1]{1,2,0:T(1,128)} %all_to_all.14), calls=%async_computation | async-start | bytes 16384 | tf_op jit(solution)/shard_map/all_to_all | solution.py:93
  22.2 2.7 fusion.11
  32.8 2.5 collective-permute-start.6
  40.6 2.8 gather_fusion
  45.0 73.5 %all-gather.5.cloned.1.call-done = bf16[2560,3072]{0,1:T(8,128)(2,1)} async-done(((bf16[2560,192]{0,1:T(8,128)(2,1)}), bf16[2560,3072]{0,1:T(8,128)(2,1)}) %all-gather.5.cloned.1.call-update) | async-done | bytes 15728656 | tf_op jit(solution)/shard_map/all_gather | solution.py:88
  118.5 13.0 %convolution_convert_fusion = bf16[512,3072]{1,0:T(8,128)(2,1)} fusion(bf16[2560,3072]{0,1:T(8,128)(2,1)} %all-gather.5.cloned.1.call-done, bf16[512,2560]{1,0:T(8,128)(2,1)S(1)} %copy-done.3, f32[2560]{0:T(1024)S(1)} %copy-done.7, f32[512]{0:T(512)S(1)} %add_rsqrt_fusion), kind=kOutput, calls=%fused_computation.24 | convolution fusion | flops 8059879424 | bytes 21508096 | tf_op jit(solution)/shard_map/dot_general | solution.py:86
  131.5 5.0 %all-to-all-start.1 = ((bf16[16,32,3072]{2,1,0:T(8,128)(2,1)}), bf16[16,32,3072]{2,1,0:T(8,128)(2,1)S(1)}, u32[]{:S(2)}, u32[]{:S(2)}) async-start(bf16[16,32,3072]{2,1,0:T(8,128)(2,1)} %bitcast.2), calls=%async_computation.1 | async-start | bytes 6291456 | tf_op jit(solution)/shard_map/all_to_all | solution.py:92
  137.4 53.5 %all-gather.7.cloned.1.call-done = bf16[1,2048,512]{2,1,0:T(8,128)(2,1)} async-done(((bf16[1,128,512]{2,1,0:T(8,128)(2,1)}), bf16[1,2048,512]{2,1,0:T(8,128)(2,1)}) %all-gather.7.cloned.1.call-update) | async-done | bytes 2097168 | tf_op jit(solution)/shard_map/all_gather | solution.py:100
  190.9 3.0 %fusion.23 = (bf16[2048,256]{1,0:T(8,128)(2,1)}, bf16[2048,256]{1,0:T(8,128)(2,1)}) fusion(bf16[2048,512]{1,0:T(8,128)(2,1)} %bitcast.69), kind=kLoop, calls=%fused_computation.55 | loop fusion | bytes 4194304 | tf_op jit(solution)/shard_map/slice | solution.py:57
  195.6 7.3 %scatter_custom_fusion = bf16[512,3072]{1,0:T(8,128)(2,1)S(1)} fusion(s32[512]{0:T(512)S(1)} %bitcast.70, bf16[512,3072]{1,0:T(8,128)(2,1)} %bitcast.67, bf16[]{:T(256)} %constant.35.clone.1), kind=kCustom, calls=%fused_computation.27 | custom fusion | bytes 3146240 | tf_op jit(solution)/shard_map/scatter | solution.py:96
  205.4 4.6 %copy.20 = bf16[1,512,2560]{1,2,0:T(8,128)(2,1)} copy(bf16[1,512,2560]{2,1,0:T(8,128)(2,1)} %slice.26) | data formatting | bytes 5242880 | tf_op jit(solution)/shard_map/slice | solution.py:104
  211.2 65.9 %while.11 = (s32[]{:T(128)}, bf16[10,512,256]{1,2,0:T(8,128)(2,1)}, bf16[10,512,256]{1,2,0:T(8,128)(2,1)}, bf16[2560,256]{1,0:T(8,128)(2,1)S(1)}, bf16[2560,256]...) while((s32[]{:T(128)}, bf16[10,512,256]{1,2,0:T(8,128)(2,1)}, ...), condition=%wide.region_5.6_spmd.clone, body=%wide.region_2.5_spmd.clone.sunk | while | flops 1357904896 | bytes 24394368 | solution.py:78
  211.3 3.2 %fusion.35 = (f32[512]{0:T(512)S(1)}, f32[512,2560]{1,0:T(8,128)S(1)}) fusion(bf16[2560,256]{1,0:T(8,128)(2,1)S(1)} %get-tuple-element.165, bf16[10,512,256]{1,2,0:T(8,128)(2,1)} %get-tuple-element.164, s32[]{:T(128)S(6)} %copy.38, pred[2560]{0:T(1024)(128)(4,1)S(1)} %get-tuple-element.168, s32[512]{0:T(512)S(1)} %get-tuple-element.167), kind=kOutput, calls=%fused_computation.54.clone.1 | convolution fusion | flops 680263168 | bytes 6822404 | tf_op jit(solution)/shard_map/while/body/eval_jaxpr/dot_general | solution.py:71
  217.8 3.2 %fusion.35 = (f32[512]{0:T(512)S(1)}, f32[512,2560]{1,0:T(8,128)S(1)}) fusion(bf16[2560,256]{1,0:T(8,128)(2,1)S(1)} %get-tuple-element.165, bf16[10,512,256]{1,2,0:T(8,128)(2,1)} %get-tuple-element.164, s32[]{:T(128)S(6)} %copy.38, pred[2560]{0:T(1024)(128)(4,1)S(1)} %get-tuple-element.168, s32[512]{0:T(512)S(1)} %get-tuple-element.167), kind=kOutput, calls=%fused_computation.54.clone.1 | convolution fusion | flops 680263168 | bytes 6822404 | tf_op jit(solution)/shard_map/while/body/eval_jaxpr/dot_general | solution.py:71
  224.4 3.2 %fusion.35 = (f32[512]{0:T(512)S(1)}, f32[512,2560]{1,0:T(8,128)S(1)}) fusion(bf16[2560,256]{1,0:T(8,128)(2,1)S(1)} %get-tuple-element.165, bf16[10,512,256]{1,2,0:T(8,128)(2,1)} %get-tuple-element.164, s32[]{:T(128)S(6)} %copy.38, pred[2560]{0:T(1024)(128)(4,1)S(1)} %get-tuple-element.168, s32[512]{0:T(512)S(1)} %get-tuple-element.167), kind=kOutput, calls=%fused_computation.54.clone.1 | convolution fusion | flops 680263168 | bytes 6822404 | tf_op jit(solution)/shard_map/while/body/eval_jaxpr/dot_general | solution.py:71
  231.0 3.2 %fusion.35 = (f32[512]{0:T(512)S(1)}, f32[512,2560]{1,0:T(8,128)S(1)}) fusion(bf16[2560,256]{1,0:T(8,128)(2,1)S(1)} %get-tuple-element.165, bf16[10,512,256]{1,2,0:T(8,128)(2,1)} %get-tuple-element.164, s32[]{:T(128)S(6)} %copy.38, pred[2560]{0:T(1024)(128)(4,1)S(1)} %get-tuple-element.168, s32[512]{0:T(512)S(1)} %get-tuple-element.167), kind=kOutput, calls=%fused_computation.54.clone.1 | convolution fusion | flops 680263168 | bytes 6822404 | tf_op jit(solution)/shard_map/while/body/eval_jaxpr/dot_general | solution.py:71
  237.6 3.2 %fusion.35 = (f32[512]{0:T(512)S(1)}, f32[512,2560]{1,0:T(8,128)S(1)}) fusion(bf16[2560,256]{1,0:T(8,128)(2,1)S(1)} %get-tuple-element.165, bf16[10,512,256]{1,2,0:T(8,128)(2,1)} %get-tuple-element.164, s32[]{:T(128)S(6)} %copy.38, pred[2560]{0:T(1024)(128)(4,1)S(1)} %get-tuple-element.168, s32[512]{0:T(512)S(1)} %get-tuple-element.167), kind=kOutput, calls=%fused_computation.54.clone.1 | convolution fusion | flops 680263168 | bytes 6822404 | tf_op jit(solution)/shard_map/while/body/eval_jaxpr/dot_general | solution.py:71
  244.2 3.2 %fusion.35 = (f32[512]{0:T(512)S(1)}, f32[512,2560]{1,0:T(8,128)S(1)}) fusion(bf16[2560,256]{1,0:T(8,128)(2,1)S(1)} %get-tuple-element.165, bf16[10,512,256]{1,2,0:T(8,128)(2,1)} %get-tuple-element.164, s32[]{:T(128)S(6)} %copy.38, pred[2560]{0:T(1024)(128)(4,1)S(1)} %get-tuple-element.168, s32[512]{0:T(512)S(1)} %get-tuple-element.167), kind=kOutput, calls=%fused_computation.54.clone.1 | convolution fusion | flops 680263168 | bytes 6822404 | tf_op jit(solution)/shard_map/while/body/eval_jaxpr/dot_general | solution.py:71
  250.8 3.2 %fusion.35 = (f32[512]{0:T(512)S(1)}, f32[512,2560]{1,0:T(8,128)S(1)}) fusion(bf16[2560,256]{1,0:T(8,128)(2,1)S(1)} %get-tuple-element.165, bf16[10,512,256]{1,2,0:T(8,128)(2,1)} %get-tuple-element.164, s32[]{:T(128)S(6)} %copy.38, pred[2560]{0:T(1024)(128)(4,1)S(1)} %get-tuple-element.168, s32[512]{0:T(512)S(1)} %get-tuple-element.167), kind=kOutput, calls=%fused_computation.54.clone.1 | convolution fusion | flops 680263168 | bytes 6822404 | tf_op jit(solution)/shard_map/while/body/eval_jaxpr/dot_general | solution.py:71
  257.4 3.2 %fusion.35 = (f32[512]{0:T(512)S(1)}, f32[512,2560]{1,0:T(8,128)S(1)}) fusion(bf16[2560,256]{1,0:T(8,128)(2,1)S(1)} %get-tuple-element.165, bf16[10,512,256]{1,2,0:T(8,128)(2,1)} %get-tuple-element.164, s32[]{:T(128)S(6)} %copy.38, pred[2560]{0:T(1024)(128)(4,1)S(1)} %get-tuple-element.168, s32[512]{0:T(512)S(1)} %get-tuple-element.167), kind=kOutput, calls=%fused_computation.54.clone.1 | convolution fusion | flops 680263168 | bytes 6822404 | tf_op jit(solution)/shard_map/while/body/eval_jaxpr/dot_general | solution.py:71
  264.0 3.2 %fusion.35 = (f32[512]{0:T(512)S(1)}, f32[512,2560]{1,0:T(8,128)S(1)}) fusion(bf16[2560,256]{1,0:T(8,128)(2,1)S(1)} %get-tuple-element.165, bf16[10,512,256]{1,2,0:T(8,128)(2,1)} %get-tuple-element.164, s32[]{:T(128)S(6)} %copy.38, pred[2560]{0:T(1024)(128)(4,1)S(1)} %get-tuple-element.168, s32[512]{0:T(512)S(1)} %get-tuple-element.167), kind=kOutput, calls=%fused_computation.54.clone.1 | convolution fusion | flops 680263168 | bytes 6822404 | tf_op jit(solution)/shard_map/while/body/eval_jaxpr/dot_general | solution.py:71
  270.6 3.2 %fusion.35 = (f32[512]{0:T(512)S(1)}, f32[512,2560]{1,0:T(8,128)S(1)}) fusion(bf16[2560,256]{1,0:T(8,128)(2,1)S(1)} %get-tuple-element.165, bf16[10,512,256]{1,2,0:T(8,128)(2,1)} %get-tuple-element.164, s32[]{:T(128)S(6)} %copy.38, pred[2560]{0:T(1024)(128)(4,1)S(1)} %get-tuple-element.168, s32[512]{0:T(512)S(1)} %get-tuple-element.167), kind=kOutput, calls=%fused_computation.54.clone.1 | convolution fusion | flops 680263168 | bytes 6822404 | tf_op jit(solution)/shard_map/while/body/eval_jaxpr/dot_general | solution.py:71
  279.4 2.8 copy.23
  (99 shorter events, 60.7 us)
Async XLA Ops:
  6.5 31.4 %copy-start.6 = (bf16[1,128,512]{2,1,0:T(8,128)(2,1)S(1)}, bf16[1,128,512]{2,1,0:T(8,128)(2,1)}, u32[]{:S(2)}) copy-start(bf16[1,128,512]{2,1,0:T(8,128)(2,1)} %param.12) | copy-start | bytes 393220
  6.5 112.0 %all-gather.5.cloned.1.call-start = ((), (), s32[]{:S(2)}) async-start(), calls=%async_computation.2 | async-start | bytes 16711680 | tf_op jit(solution)/shard_map/all_gather | solution.py:88
  7.3 12.9 %collective-permute-start = (bf16[1,128,512]{2,1,0:T(8,128)(2,1)}, bf16[1,128,512]{2,1,0:T(8,128)(2,1)S(1)}, u32[]{:S(2)}, u32[]{:S(2)}) collective-permute-start(bf16[1,128,512]{2,1,0:T(8,128)(2,1)} %param.12), channel_id=1, source_target_pairs={{0,16},{16,32},{32,48},{48,64},{64,80},{80,96},{96,112},{112,0},{1... | collective-permute-start | bytes 393224 | tf_op jit(solution)/shard_map/ppermute | solution.py:35
  9.9 16.6 %collective-permute-start.4 = (bf16[1,128,512]{2,1,0:T(8,128)(2,1)}, bf16[1,128,512]{2,1,0:T(8,128)(2,1)S(1)}, u32[]{:S(2)}, u32[]{:S(2)}) collective-permute-start(bf16[1,128,512]{2,1,0:T(8,128)(2,1)} %param.12), channel_id=1, source_target_pairs={{16,0},{32,16},{48,32},{64,48},{80,64},{96,80},{112,96},{0,112},{1... | collective-permute-start | bytes 393224 | tf_op jit(solution)/shard_map/ppermute | solution.py:38
  12.5 119.1 %all-to-all-start = ((s32[16,32,1]{1,2,0:T(1,128)}), s32[16,32,1]{1,2,0:T(1,128)S(1)}, u32[]{:S(2)}, u32[]{:S(2)}) async-start(s32[16,32,1]{1,2,0:T(1,128)} %all_to_all.14), calls=%async_computation | async-start | bytes 16384 | tf_op jit(solution)/shard_map/all_to_all | solution.py:93
  20.1 170.8 %all-gather.7.cloned.1.call-start = ((), (), s32[]{:S(2)}) async-start(), calls=%async_computation.3 | async-start | bytes 2228224 | tf_op jit(solution)/shard_map/all_gather | solution.py:100
  20.2 4.7 %collective-permute-start.1 = (bf16[1,128,512]{2,1,0:T(8,128)(2,1)S(1)}, bf16[1,128,512]{2,1,0:T(8,128)(2,1)S(1)}, u32[]{:S(2)}, u32[]{:S(2)}) collective-permute-start(bf16[1,128,512]{2,1,0:T(8,128)(2,1)S(1)} %collective-permute-done), channel_id=1, source_target_pairs={{0,16},{16,32},{32,48},{48,64},{64,80},{80,96},{96,112},{112,0},{1... | collective-permute-start | bytes 393224 | tf_op jit(solution)/shard_map/ppermute | solution.py:35
  24.9 93.7 %copy-start.3 = (bf16[512,2560]{1,0:T(8,128)(2,1)S(1)}, bf16[512,2560]{1,0:T(8,128)(2,1)}, u32[]{:S(2)}) copy-start(bf16[512,2560]{1,0:T(8,128)(2,1)} %param.9) | copy-start | bytes 7864324
  24.9 3.8 %collective-permute-start.2 = (bf16[1,128,512]{2,1,0:T(8,128)(2,1)S(1)}, bf16[1,128,512]{2,1,0:T(8,128)(2,1)S(1)}, u32[]{:S(2)}, u32[]{:S(2)}) collective-permute-start(bf16[1,128,512]{2,1,0:T(8,128)(2,1)S(1)} %collective-permute-done.1), channel_id=1, source_target_pairs={{0,16},{16,32},{32,48},{48,64},{64,80},{80,96},{96,112},{112,0},{1... | collective-permute-start | bytes 393224 | tf_op jit(solution)/shard_map/ppermute | solution.py:35
  26.6 6.2 %collective-permute-start.5 = (bf16[1,128,512]{2,1,0:T(8,128)(2,1)S(1)}, bf16[1,128,512]{2,1,0:T(8,128)(2,1)S(1)}, u32[]{:S(2)}, u32[]{:S(2)}) collective-permute-start(bf16[1,128,512]{2,1,0:T(8,128)(2,1)S(1)} %collective-permute-done.4), channel_id=1, source_target_pairs={{16,0},{32,16},{48,32},{64,48},{80,64},{96,80},{112,96},{0,112},{1... | collective-permute-start | bytes 393224 | tf_op jit(solution)/shard_map/ppermute | solution.py:38
  28.7 6.6 %collective-permute-start.3 = (bf16[1,128,512]{2,1,0:T(8,128)(2,1)S(1)}, bf16[1,128,512]{2,1,0:T(8,128)(2,1)S(1)}, u32[]{:S(2)}, u32[]{:S(2)}) collective-permute-start(bf16[1,128,512]{2,1,0:T(8,128)(2,1)S(1)} %collective-permute-done.2), channel_id=1, source_target_pairs={{0,16},{16,32},{32,48},{48,64},{64,80},{80,96},{96,112},{112,0},{1... | collective-permute-start | bytes 393224 | tf_op jit(solution)/shard_map/ppermute | solution.py:35
  32.8 7.1 %collective-permute-start.6 = (bf16[1,128,512]{2,1,0:T(8,128)(2,1)S(1)}, bf16[1,128,512]{2,1,0:T(8,128)(2,1)S(1)}, u32[]{:S(2)}, u32[]{:S(2)}) collective-permute-start(bf16[1,128,512]{2,1,0:T(8,128)(2,1)S(1)} %collective-permute-done.5), channel_id=1, source_target_pairs={{16,0},{32,16},{48,32},{64,48},{80,64},{96,80},{112,96},{0,112},{1... | collective-permute-start | bytes 393224 | tf_op jit(solution)/shard_map/ppermute | solution.py:38
  35.9 82.6 %copy-start.7 = (f32[2560]{0:T(1024)S(1)}, f32[2560]{0:T(1024)}, u32[]{:S(2)}) copy-start(f32[2560]{0:T(1024)} %param.10) | copy-start | bytes 30724
  131.5 62.4 %all-to-all-start.1 = ((bf16[16,32,3072]{2,1,0:T(8,128)(2,1)}), bf16[16,32,3072]{2,1,0:T(8,128)(2,1)S(1)}, u32[]{:S(2)}, u32[]{:S(2)}) async-start(bf16[16,32,3072]{2,1,0:T(8,128)(2,1)} %bitcast.2), calls=%async_computation.1 | async-start | bytes 6291456 | tf_op jit(solution)/shard_map/all_to_all | solution.py:92
  193.9 1.6 copy-start.2
  205.4 4.6 %copy-start.4 = (bf16[512,512]{1,0:T(8,128)(2,1)S(1)}, bf16[512,512]{1,0:T(8,128)(2,1)}, u32[]{:S(2)}) copy-start(bf16[512,512]{1,0:T(8,128)(2,1)} %slice_bitcast_fusion) | copy-start | bytes 1572868
  205.4 4.6 %copy-start = (bf16[2048,256]{1,0:T(8,128)(2,1)S(1)}, bf16[2048,256]{1,0:T(8,128)(2,1)}, u32[]{:S(2)}) copy-start(bf16[2048,256]{1,0:T(8,128)(2,1)} %get-tuple-element.93) | copy-start | bytes 3145732
  205.4 4.6 %copy-start.1 = (bf16[2048,256]{1,0:T(8,128)(2,1)S(1)}, bf16[2048,256]{1,0:T(8,128)(2,1)}, u32[]{:S(2)}) copy-start(bf16[2048,256]{1,0:T(8,128)(2,1)} %get-tuple-element.94) | copy-start | bytes 3145732
  214.5 1.3 copy-start.5
  221.1 1.3 copy-start.5
  227.7 1.3 copy-start.5
  234.3 1.3 copy-start.5
  240.9 1.3 copy-start.5
  247.5 1.3 copy-start.5
  (4 other events, 5.3 us)
Sparse Core Ops, SparseCore 0:
  9.5 108.9 all-gather.4
  120.7 70.1 all-gather.6
